TPU v7x, 32 devices: a whole 2x2x4 slice. The times are simulated.
32 devices in a mesh: rep: 4 (over y, core), shard: 8 (over z, x).
Axes of the slice: x: 2, y: 2, z: 4, core: 2. Of those that a mesh axis runs over, the one named last changes fastest.
Arguments:
- cell_features: bfloat16 [4, 4096, 1024], P('rep', 'shard'), may hold values from -10 to 10
- upstream: bfloat16 [4, 4096, 1024], P('rep', 'shard'), may hold values from -0.119628906 to 0.119628906
- qkv_weight: bfloat16 [4, 1024, 3072], P('rep', 'shard'), may hold values from -0.1875 to 0.1875
- out_weight: bfloat16 [4, 1024, 1024], P('rep', 'shard'), may hold values from -0.1875 to 0.1875
- momentum: float32 [4, 1024, 1024], P('rep', 'shard'), may hold values from -4 to 4
- key_tiles: int32 [4, 32, 6], P('rep'), may hold values from 0 to 31, as said below
- live_blocks: int32 [4, 32], P('rep'), may hold values from 1 to 6
- step_index: int32 [], replicated, may hold values from 0 to 999
Outputs:
- layer_out: bfloat16 [4, 4096, 1024], P('rep', 'shard')
- new_weight: bfloat16 [4, 1024, 1024], P('rep', 'shard')
- new_momentum: float32 [4, 1024, 1024], P('rep', 'shard')
Inputs may be any that keep to these rules, and one draw needn't show every extreme that they name: `key_tiles`: every entry names a tile of its group. Of the 24 entries of device d's 4 query tiles (tiles d*4 to (d+1)*4 - 1), exactly 12 name tiles of device d itself (tile // 4 == d); of the others at most 2 name tiles of any one other device, and in every draw some device is named exactly 2 times.
All inputs are finite; a program needn't handle non-finite values.
Results may differ from a plain program's by a relative error of at most 0.025.
Values may be sent and summed in bfloat16 or wider, within the bound.
No kernel may reach another device: no remote copies, remote signals or barrier semaphores. Data moves between devices by JAX's collectives and lax.ppermute only.
A program may use at most 128 MiB of HBM per device.

v0:
```python
import functools
import jax
import jax.numpy as jnp
from jax import lax
from jax.sharding import PartitionSpec as P

HEADS = 16
HEAD_DIM = 64
TILE = 128
KB = 6
momentum_beta = 0.9


def shortened(value):

    def short(part):
        return part.astype(jnp.bfloat16) if part.dtype == jnp.float32 else part

    return jax.tree.map(short, value)


def partner(value, axis, bit):
    return lax.ppermute(value, axis, [(i, i ^ 1 << bit) for i in range(lax.axis_size(axis))])


def add_rows(source, shard_rows):
    return jnp.dot(source, shard_rows, preferred_element_type=jnp.float32)


def attend_tile(local_table, arrived_table, element):
    query_tile, is_remote, local_index, arrive_index, live_count = element
    model_width = query_tile.shape[1]
    from_local = local_table[local_index]
    from_remote = arrived_table[arrive_index]
    key_value = jnp.where(is_remote[:, None, None], from_remote, from_local).reshape(
        KB * TILE, 2 * model_width
    )
    query_split = query_tile.reshape(TILE, HEADS, HEAD_DIM)
    keys_split = key_value[:, :model_width].reshape(KB * TILE, HEADS, HEAD_DIM)
    values_split = key_value[:, model_width:].reshape(KB * TILE, HEADS, HEAD_DIM)
    scores = jnp.einsum(
        "qhd,khd->hqk", query_split, keys_split, preferred_element_type=jnp.float32
    ) * HEAD_DIM ** (-0.5)
    usable = jnp.arange(KB * TILE, dtype=jnp.int32) // TILE < live_count
    scores = jnp.where(usable[None, None, :], scores, jnp.float32(-1e30))
    row_max = jnp.max(scores, axis=2, keepdims=True)
    exponent = jnp.exp(scores - row_max)
    probabilities = (exponent / jnp.sum(exponent, axis=2, keepdims=True)).astype(jnp.bfloat16)
    mixture = jnp.einsum(
        "hqk,khd->qhd", probabilities, values_split, preferred_element_type=jnp.float32
    )
    return mixture.reshape(TILE, model_width).astype(jnp.bfloat16)


def swap_with(bit_number, stacked_pair):
    return jax.tree.map(
        lambda part, own: part.astype(own.dtype),
        partner(shortened(stacked_pair), "rep", bit_number),
        stacked_pair,
    )


def body(
    cell_features, upstream, qkv_weight, out_weight, momentum, key_tiles, live_blocks, step_index
):
    features = cell_features[0]
    row_count, model_width = features.shape
    tile_count = row_count // TILE
    shard_count = lax.axis_size("shard")
    my_index = lax.axis_index("shard")
    slot_count = tile_count * KB
    remote_count = slot_count - slot_count // 2
    capacity = (remote_count + shard_count - 2) // (shard_count - 1)
    requests = key_tiles[0].reshape(shard_count, slot_count)
    owners = requests // tile_count
    local_tile = requests % tile_count
    requester = jnp.arange(shard_count, dtype=jnp.int32)[:, None]
    elsewhere = owners != requester
    positions = jnp.arange(slot_count, dtype=jnp.int32)
    earlier = positions[None, :] < positions[:, None]
    same_owner = owners[:, :, None] == owners[:, None, :]
    owner_rank = jnp.sum((same_owner & earlier[None]).astype(jnp.int32), axis=2)
    owned = (owners == my_index) & elsewhere
    slot_ids = jnp.arange(capacity, dtype=jnp.int32)
    chosen = owned[:, :, None] & (owner_rank[:, :, None] == slot_ids[None, None, :])
    send_index = jnp.sum(chosen.astype(jnp.int32) * local_tile[:, :, None], axis=1).reshape(-1)
    send_valid = jnp.any(chosen, axis=1).reshape(-1)
    my_owners = lax.dynamic_index_in_dim(owners, my_index, 0, keepdims=False)
    my_ranks = lax.dynamic_index_in_dim(owner_rank, my_index, 0, keepdims=False)
    my_local = lax.dynamic_index_in_dim(local_tile, my_index, 0, keepdims=False)
    my_remote = my_owners != my_index
    arrive_index = jnp.where(my_remote, my_owners * capacity + my_ranks, 0)
    local_index = jnp.where(my_remote, 0, my_local)
    projected = add_rows(
        features, lax.all_gather(qkv_weight[0], "shard", axis=0, tiled=True)
    ).astype(jnp.bfloat16)
    picked = projected[:, model_width:].reshape(tile_count, TILE, 2 * model_width)[send_index]
    sent = jnp.where(send_valid[:, None, None], picked, jnp.zeros_like(picked)).reshape(
        shard_count, capacity, TILE, 2 * model_width
    )
    arrived = lax.all_to_all(sent, "shard", split_axis=0, concat_axis=0, tiled=True)
    arrived_table = arrived.reshape(shard_count * capacity, TILE, 2 * model_width)
    query = projected[:, :model_width].reshape(tile_count, TILE, model_width)
    local_table = projected[:, model_width:].reshape(tile_count, TILE, 2 * model_width)
    live_mine = lax.dynamic_slice_in_dim(live_blocks[0], my_index * tile_count, tile_count, 0)
    per_tile = functools.partial(attend_tile, local_table, arrived_table)
    elements = (
        query,
        my_remote.reshape(tile_count, KB),
        local_index.reshape(tile_count, KB),
        arrive_index.reshape(tile_count, KB),
        live_mine,
    )
    attended = lax.map(per_tile, elements).reshape(row_count, model_width)
    product = add_rows(attended, lax.all_gather(out_weight[0], "shard", axis=0, tiled=True))
    layer_out = (features.astype(jnp.float32) + product).astype(jnp.bfloat16)
    gradient = lax.psum_scatter(
        lax.dot_general(
            attended, upstream[0], (((0,), (0,)), ((), ())), preferred_element_type=jnp.float32
        ).astype(jnp.bfloat16),
        "shard",
        scatter_dimension=0,
        tiled=True,
    ).astype(jnp.float32)
    learn_rate = jnp.float32(50.0) / (jnp.float32(500.0) + step_index.astype(jnp.float32))
    velocity = momentum_beta * momentum[0] + gradient
    stepped = (out_weight[0].astype(jnp.float32) - learn_rate * velocity).astype(jnp.bfloat16)
    stacked_pair = jnp.stack([stepped.astype(jnp.float32), velocity])
    bit_count = lax.axis_size("rep").bit_length() - 1
    branches = [functools.partial(swap_with, bit_number) for bit_number in range(bit_count)]
    bit_choice = step_index % bit_count
    partner_pair = lax.switch(bit_choice, branches, stacked_pair)
    averaged = 0.5 * (stacked_pair + partner_pair)
    new_weight = averaged[0].astype(jnp.bfloat16)
    new_momentum = averaged[1]
    return (layer_out[None], new_weight[None], new_momentum[None])


def solution(mesh):
    placed = (
        P("rep", "shard", None),
        P("rep", "shard", None),
        P("rep", "shard", None),
        P("rep", "shard", None),
        P("rep", "shard", None),
        P("rep", None, None),
        P("rep", None),
        P(),
    )
    return jax.shard_map(
        body,
        mesh=mesh,
        in_specs=placed,
        out_specs=(P("rep", "shard", None), P("rep", "shard", None), P("rep", "shard", None)),
        check_vma=False,
    )
```

profile of v0, /device:TPU:0, one launch (start us, length us, event | category | flops | bytes accessed | tf_op | source)
XLA Modules:
  0.0 585.2 jit_solution(10328500597849223528)
XLA Ops:
  7.9 0.8 copy.21
  9.7 101.9 %all-gather.5.cloned.1.call-done = bf16[1,1024,3072]{2,1,0:T(8,128)(2,1)} async-done(((bf16[1,128,3072]{2,1,0:T(8,128)(2,1)}), bf16[1,1024,3072]{2,1,0:T(8,128)(2,1)}) %all-gather.5.cloned.1.call-update) | async-done | bytes 6291472 | tf_op jit(solution)/shard_map/all_gather | solution.py:95
  111.6 6.5 %fusion.21 = bf16[512,3072]{1,0:T(8,128)(2,1)S(1)} fusion(bf16[1,1024,3072]{2,1,0:T(8,128)(2,1)} %all-gather.5.cloned.1.call-done, bf16[1,512,1024]{2,1,0:T(8,128)(2,1)} %param.12), kind=kOutput, calls=%fused_computation.42 | convolution fusion | flops 3222798336 | bytes 10485760 | tf_op jit(solution)/shard_map/dot_general | solution.py:27
  118.2 1.6 copy-done.1
  120.0 4.6 gather_fusion.2
  124.7 7.2 %broadcast_select_fusion.1 = bf16[8,2,128,2048]{3,2,1,0:T(8,128)(2,1)} fusion(bf16[8,2,128,2048]{3,2,1,0:T(8,128)(2,1)} %bitcast.120, pred[8,2]{1,0:T(8,128)(4,1)S(1)} %copy.22), kind=kLoop, calls=%fused_computation.39 | loop fusion | flops 4194304 | bytes 16777232 | tf_op jit(solution)/shard_map/jit(_where)/select_n | solution.py:98
  131.9 5.1 all-to-all-start
  138.3 2.3 slice.39
  140.6 203.7 %all-to-all-done = bf16[8,2,128,2048]{3,2,1,0:T(8,128)(2,1)} async-done(((bf16[8,2,128,2048]{3,2,1,0:T(8,128)(2,1)}), bf16[8,2,128,2048]{3,2,1,0:T(8,128)(2,1)}, u32[]{:S(2)}, u32[]{:S(2)}) %all-to-all-start) | async-done | bytes 8388640 | tf_op jit(solution)/shard_map/all_to_all | solution.py:101
  344.3 157.9 %while.12 = (s32[]{:T(128)}, bf16[4,128,1024]{2,1,0:T(8,128)(2,1)}, pred[4,6]{1,0:T(4,128)(4,1)S(1)}, s32[4,6]{1,0:T(4,128)S(1)}, bf16[16,128,2048]{2,1,0:T(8,12...) while((s32[]{:T(128)}, bf16[4,128,1024]{2,1,0:T(8,128)(2,1)}, ...), condition=%wide.region_6.7_spmd, body=%wide.region_3.6_spmd.sunk | while | flops 413804064 | bytes 59273044 | solution.py:114
  344.3 6.0 %gather_fusion = bf16[6,128,2048]{2,1,0:T(8,128)(2,1)} fusion(bf16[16,128,2048]{2,1,0:T(8,128)(2,1)} %get-tuple-element.279, s32[1024]{0:T(1024)S(1)} %pad_clamp_fusion.5), kind=kCustom, calls=%fused_computation.clone.1 | custom fusion | bytes 6291480 | tf_op jit(solution)/shard_map/while/body/eval_jaxpr/gather | solution.py:34
  350.3 4.7 copy.33
  355.0 2.5 gather_fusion.1
  357.4 4.6 copy.34
  362.2 3.2 broadcast_select_fusion.5
  365.4 1.8 fusion.68
  367.2 1.0 constant_dynamic-slice_fusion.8
  368.1 0.8 copy.35
  370.3 6.4 %fusion.70 = (f32[16,128]{1,0:T(8,128)S(1)}, f32[16,128,768]{2,1,0:T(8,128)}) fusion(pred[768]{0:T(1024)(128)(4,1)S(1)} %fusion.69, bf16[128,16,64]{0,2,1:T(8,128)(2,1)} %bitcast.121, bf16[768,16,64]{0,2,1:T(8,128)(2,1)} %bitcast.119), kind=kOutput, calls=%fused_computation.90.clone.1 | convolution fusion | flops 207618816 | bytes 8135424 | tf_op jit(solution)/shard_map/while/body/eval_jaxpr/sub | solution.py:47
  376.7 5.3 fusion.71
  381.9 1.1 copy.36
  383.8 6.0 %gather_fusion = bf16[6,128,2048]{2,1,0:T(8,128)(2,1)} fusion(bf16[16,128,2048]{2,1,0:T(8,128)(2,1)} %get-tuple-element.279, s32[1024]{0:T(1024)S(1)} %pad_clamp_fusion.5), kind=kCustom, calls=%fused_computation.clone.1 | custom fusion | bytes 6291480 | tf_op jit(solution)/shard_map/while/body/eval_jaxpr/gather | solution.py:34
  389.8 4.7 copy.33
  394.4 2.5 gather_fusion.1
  396.9 4.6 copy.34
  401.6 3.2 broadcast_select_fusion.5
  404.8 1.8 fusion.68
  406.6 1.0 constant_dynamic-slice_fusion.8
  407.6 0.8 copy.35
  409.7 6.4 %fusion.70 = (f32[16,128]{1,0:T(8,128)S(1)}, f32[16,128,768]{2,1,0:T(8,128)}) fusion(pred[768]{0:T(1024)(128)(4,1)S(1)} %fusion.69, bf16[128,16,64]{0,2,1:T(8,128)(2,1)} %bitcast.121, bf16[768,16,64]{0,2,1:T(8,128)(2,1)} %bitcast.119), kind=kOutput, calls=%fused_computation.90.clone.1 | convolution fusion | flops 207618816 | bytes 8135424 | tf_op jit(solution)/shard_map/while/body/eval_jaxpr/sub | solution.py:47
  416.1 5.3 fusion.71
  421.4 1.1 copy.36
  422.5 0.7 constant_dynamic-update-slice_fusion.2
  423.3 6.0 %gather_fusion = bf16[6,128,2048]{2,1,0:T(8,128)(2,1)} fusion(bf16[16,128,2048]{2,1,0:T(8,128)(2,1)} %get-tuple-element.279, s32[1024]{0:T(1024)S(1)} %pad_clamp_fusion.5), kind=kCustom, calls=%fused_computation.clone.1 | custom fusion | bytes 6291480 | tf_op jit(solution)/shard_map/while/body/eval_jaxpr/gather | solution.py:34
  429.2 4.7 copy.33
  433.9 2.5 gather_fusion.1
  436.4 4.6 copy.34
  441.1 3.2 broadcast_select_fusion.5
  444.3 1.8 fusion.68
  446.1 1.0 constant_dynamic-slice_fusion.8
  447.1 0.8 copy.35
  449.2 6.4 %fusion.70 = (f32[16,128]{1,0:T(8,128)S(1)}, f32[16,128,768]{2,1,0:T(8,128)}) fusion(pred[768]{0:T(1024)(128)(4,1)S(1)} %fusion.69, bf16[128,16,64]{0,2,1:T(8,128)(2,1)} %bitcast.121, bf16[768,16,64]{0,2,1:T(8,128)(2,1)} %bitcast.119), kind=kOutput, calls=%fused_computation.90.clone.1 | convolution fusion | flops 207618816 | bytes 8135424 | tf_op jit(solution)/shard_map/while/body/eval_jaxpr/sub | solution.py:47
  455.6 5.3 fusion.71
  460.9 1.1 copy.36
  462.0 0.7 constant_dynamic-update-slice_fusion.2
  462.8 6.0 %gather_fusion = bf16[6,128,2048]{2,1,0:T(8,128)(2,1)} fusion(bf16[16,128,2048]{2,1,0:T(8,128)(2,1)} %get-tuple-element.279, s32[1024]{0:T(1024)S(1)} %pad_clamp_fusion.5), kind=kCustom, calls=%fused_computation.clone.1 | custom fusion | bytes 6291480 | tf_op jit(solution)/shard_map/while/body/eval_jaxpr/gather | solution.py:34
  468.7 4.7 copy.33
  473.4 2.5 gather_fusion.1
  475.9 4.6 copy.34
  480.6 3.2 broadcast_select_fusion.5
  483.8 1.8 fusion.68
  485.6 1.0 constant_dynamic-slice_fusion.8
  486.6 0.8 copy.35
  488.7 6.4 %fusion.70 = (f32[16,128]{1,0:T(8,128)S(1)}, f32[16,128,768]{2,1,0:T(8,128)}) fusion(pred[768]{0:T(1024)(128)(4,1)S(1)} %fusion.69, bf16[128,16,64]{0,2,1:T(8,128)(2,1)} %bitcast.121, bf16[768,16,64]{0,2,1:T(8,128)(2,1)} %bitcast.119), kind=kOutput, calls=%fused_computation.90.clone.1 | convolution fusion | flops 207618816 | bytes 8135424 | tf_op jit(solution)/shard_map/while/body/eval_jaxpr/sub | solution.py:47
  495.1 5.3 fusion.71
  500.4 1.1 copy.36
  502.2 3.9 convolution_convert_fusion
  506.9 4.2 fusion.28
  511.1 62.4 %reduce-scatter.2.cloned.1.call-done = bf16[128,1024]{1,0:T(8,128)(2,1)} async-done(((bf16[1024,1024]{1,0:T(8,128)(2,1)}), bf16[128,1024]{1,0:T(8,128)(2,1)}) %reduce-scatter.2.cloned.1.call-update) | async-done | bytes 262160 | tf_op jit(solution)/shard_map/reduce_scatter | solution.py:117
  573.6 1.1 fusion.36
  574.7 2.1 conditional.4
  574.8 1.9 collective-permute-done
  577.1 0.8 slice.41
  577.9 0.7 slice.43
  (73 shorter events, 10.7 us)
Async XLA Ops:
  7.2 495.0 %copy-start = (bf16[1,512,1024]{2,1,0:T(8,128)(2,1)S(1)}, bf16[1,512,1024]{2,1,0:T(8,128)(2,1)}, u32[]{:S(2)}) copy-start(bf16[1,512,1024]{2,1,0:T(8,128)(2,1)} %param.13) | copy-start | bytes 3145732
  7.2 104.4 %all-gather.5.cloned.1.call-start = ((), (), s32[]{:S(2)}) async-start(), calls=%async_computation.3 | async-start | bytes 7077888 | tf_op jit(solution)/shard_map/all_gather | solution.py:95
  118.2 1.7 copy-start.1
  131.9 6.4 %copy-start.5 = (s32[1,32]{1,0:T(1,128)S(1)}, s32[1,32]{1,0:T(1,128)}, u32[]{:S(2)}) copy-start(s32[1,32]{1,0:T(1,128)} %param.18) | copy-start | bytes 388
  131.9 212.4 %all-to-all-start = ((bf16[8,2,128,2048]{3,2,1,0:T(8,128)(2,1)}), bf16[8,2,128,2048]{3,2,1,0:T(8,128)(2,1)}, u32[]{:S(2)}, u32[]{:S(2)}) async-start(bf16[8,2,128,2048]{3,2,1,0:T(8,128)(2,1)} %broadcast_select_fusion.1), calls=%async_computation | async-start | bytes 16777216 | tf_op jit(solution)/shard_map/all_to_all | solution.py:101
  136.9 370.0 %all-gather.7.cloned.1.call-start = ((), (), s32[]{:S(2)}) async-start(), calls=%async_computation.4 | async-start | bytes 2359296 | tf_op jit(solution)/shard_map/all_gather | solution.py:115
  137.7 435.9 %reduce-scatter.2.cloned.1.call-start = ((), (), s32[]{:S(2)}) async-start(), calls=%async_computation.2 | async-start | bytes 2359296 | tf_op jit(solution)/shard_map/reduce_scatter | solution.py:117
  502.2 4.7 copy-start.4
  506.9 66.7 %copy-start.2 = (bf16[1,128,1024]{2,1,0:T(8,128)(2,1)S(1)}, bf16[1,128,1024]{2,1,0:T(8,128)(2,1)}, u32[]{:S(2)}) copy-start(bf16[1,128,1024]{2,1,0:T(8,128)(2,1)} %param.15) | copy-start | bytes 786436
  506.9 66.7 %copy-start.3 = (f32[1,128,1024]{2,1,0:T(8,128)S(1)}, f32[1,128,1024]{2,1,0:T(8,128)}, u32[]{:S(2)}) copy-start(f32[1,128,1024]{2,1,0:T(8,128)} %param.16) | copy-start | bytes 1572868
  574.8 2.0 collective-permute-start
Sparse Core Ops, SparseCore 0:
  10.2 101.3 all-gather.4
  139.9 169.2 all-gather.6
  506.3 67.2 reduce-scatter.1
where the time goes:
time: 587 us; the launch traced here: 585 us
  waiting for transfers between devices  371 us (63%)
  local copies, waits for them, and re-layouts  108 us (18%)
  matrix products  61.4 us (10%)
  other arithmetic  24.6 us (4%)
  between operations  14.6 us (2%)
    all_to_all x1, waiting for transfers between devices, body(): lax.all_to_all(sent, 'shard', split_axis=0, concat_axis=0, tiled=True)  204 us
    all_gather x1, waiting for transfers between devices, body(): lax.all_gather(qkv_weight[0], 'shard', axis=0, tiled=True)  102 us
    reduce_scatter x1, waiting for transfers between devices, body(): lax.psum_scatter(lax.dot_general(attended, upstream[0], (((0,), (0,)), ((...  62.4 us
    gather x8, local copies, waits for them, and re-layouts, attend_tile(): from_remote = arrived_table[arrive_index]  42.6 us
    gather x8, local copies, waits for them, and re-layouts, attend_tile(): from_local = local_table[local_index]  28.5 us
    sub x4, matrix products, attend_tile(): exponent = jnp.exp(scores - row_max)  25.6 us
    dot_general x4, matrix products, attend_tile(): jnp.einsum('hqk,khd->qhd', probabilities, values_split, preferred_element...  21.1 us
    select_n x4, other arithmetic, attend_tile(): jnp.where(is_remote[:, None, None], from_remote, from_local)  12.7 us
  transfers between devices with their start and end apart: 5, of which 4 were waited for; matrix products, arithmetic and copies ran while one was open for 29% of the time, Pallas kernels for 0%

commit v1 on v0

--- a/solution.py
+++ b/solution.py
@@ -9,6 +9,33 @@
 TILE = 128
 KB = 6
 momentum_beta = 0.9
+
+
+def scenes_put(local_block, dimension_no):
+    value_now, q_next, res = (
+        lax.axis_size("shard"),
+        lax.axis_index("shard"),
+        local_block.shape[dimension_no],
+    )
+    runs = list(map(lambda i0: (i0, (i0 + 1) % value_now), range(value_now)))
+    b_next = local_block
+    w2 = jnp.zeros(
+        (
+            *local_block.shape[:dimension_no],
+            value_now * res,
+            *local_block.shape[dimension_no + 1 :],
+        ),
+        local_block.dtype,
+    )
+    for nth in range(value_now):
+        prior = (q_next - nth) % value_now
+        w2 = lax.dynamic_update_slice_in_dim(w2, b_next, prior * res, axis=dimension_no)
+        if nth < value_now - 1:
+            b_next = lax.ppermute(b_next, "shard", runs)
+    return w2
+
+
+finish_the_body = functools.partial(scenes_put, dimension_no=0)
 
 
 def shortened(value):
@@ -91,9 +118,7 @@
     my_remote = my_owners != my_index
     arrive_index = jnp.where(my_remote, my_owners * capacity + my_ranks, 0)
     local_index = jnp.where(my_remote, 0, my_local)
-    projected = add_rows(
-        features, lax.all_gather(qkv_weight[0], "shard", axis=0, tiled=True)
-    ).astype(jnp.bfloat16)
+    projected = add_rows(features, finish_the_body(qkv_weight[0])).astype(jnp.bfloat16)
     picked = projected[:, model_width:].reshape(tile_count, TILE, 2 * model_width)[send_index]
     sent = jnp.where(send_valid[:, None, None], picked, jnp.zeros_like(picked)).reshape(
         shard_count, capacity, TILE, 2 * model_width

time: 587 us -> 615 us (1.048)
  waiting for transfers between devices: 371 us -> 395 us
    ppermute x0 -> x7, waiting for transfers between devices: none -> 132 us  [scenes_put(): b_next = lax.ppermute(b_next, 'shard', runs)]
    all_gather x1 -> x0, waiting for transfers between devices: 102 us -> none  [body(): lax.all_gather(qkv_weight[0], 'shard', axis=0, tiled=True)]
  transfers between devices with their start and end apart: 5 -> 11, of which waited for: 4 -> 10; matrix products, arithmetic and copies ran while one was open for 29% -> 28% of each run, Pallas kernels for 0% -> 0%
where the time goes in v1:
time: 615 us; the launch traced here: 613 us
  waiting for transfers between devices  395 us (64%)
  local copies, waits for them, and re-layouts  111 us (18%)
  matrix products  58.4 us (9%)
  other arithmetic  24.7 us (4%)
  between operations  15.1 us (2%)
  starting transfers between devices  8.43 us (1%)
    all_to_all x1, waiting for transfers between devices, body(): lax.all_to_all(sent, 'shard', split_axis=0, concat_axis=0, tiled=True)  199 us
    ppermute x7, waiting for transfers between devices, scenes_put(): b_next = lax.ppermute(b_next, 'shard', runs)  132 us
    reduce_scatter x1, waiting for transfers between devices, body(): lax.psum_scatter(lax.dot_general(attended, upstream[0], (((0,), (0,)), ((...  61.7 us
    gather x8, local copies, waits for them, and re-layouts, attend_tile(): from_remote = arrived_table[arrive_index]  42.7 us
    gather x8, local copies, waits for them, and re-layouts, attend_tile(): from_local = local_table[local_index]  28.5 us
    sub x4, matrix products, attend_tile(): exponent = jnp.exp(scores - row_max)  25.5 us
    dot_general x4, matrix products, attend_tile(): jnp.einsum('hqk,khd->qhd', probabilities, values_split, preferred_element...  21.1 us
    select_n x4, other arithmetic, attend_tile(): jnp.where(is_remote[:, None, None], from_remote, from_local)  12.7 us
  transfers between devices with their start and end apart: 11, of which 10 were waited for; matrix products, arithmetic and copies ran while one was open for 28% of the time, Pallas kernels for 0%

profile of v1, /device:TPU:0, one launch (start us, length us, event | category | flops | bytes accessed | tf_op | source)
XLA Modules:
  0.0 613.1 jit_solution(6889668086939195370)
XLA Ops:
  7.2 3.0 collective-permute-start.2
  10.2 20.8 %collective-permute-done.2 = bf16[128,3072]{1,0:T(8,128)(2,1)S(1)} collective-permute-done((bf16[128,3072]{1,0:T(8,128)(2,1)}, bf16[128,3072]{1,0:T(8,128)(2,1)S(1)}, u32[]{:S(2)}, u32[]{:S(2)}) %collective-permute-start.2) | collective-permute-done | bytes 786464 | tf_op jit(solution)/shard_map/ppermute | solution.py:34
  31.0 21.4 %collective-permute-done.3 = bf16[128,3072]{1,0:T(8,128)(2,1)S(1)} collective-permute-done((bf16[128,3072]{1,0:T(8,128)(2,1)S(1)}, bf16[128,3072]{1,0:T(8,128)(2,1)S(1)}, u32[]{:S(2)}, u32[]{:S(2)}) %collective-permute-start.3) | collective-permute-done | bytes 786464 | tf_op jit(solution)/shard_map/ppermute | solution.py:34
  53.3 19.8 %collective-permute-done.4 = bf16[128,3072]{1,0:T(8,128)(2,1)} collective-permute-done((bf16[128,3072]{1,0:T(8,128)(2,1)S(1)}, bf16[128,3072]{1,0:T(8,128)(2,1)}, u32[]{:S(2)}, u32[]{:S(2)}) %collective-permute-start.4) | collective-permute-done | bytes 786464 | tf_op jit(solution)/shard_map/ppermute | solution.py:34
  73.9 19.1 %collective-permute-done.5 = bf16[128,3072]{1,0:T(8,128)(2,1)} collective-permute-done((bf16[128,3072]{1,0:T(8,128)(2,1)}, bf16[128,3072]{1,0:T(8,128)(2,1)}, u32[]{:S(2)}, u32[]{:S(2)}) %collective-permute-start.5) | collective-permute-done | bytes 786464 | tf_op jit(solution)/shard_map/ppermute | solution.py:34
  94.0 18.1 %collective-permute-done.6 = bf16[128,3072]{1,0:T(8,128)(2,1)S(1)} collective-permute-done((bf16[128,3072]{1,0:T(8,128)(2,1)}, bf16[128,3072]{1,0:T(8,128)(2,1)S(1)}, u32[]{:S(2)}, u32[]{:S(2)}) %collective-permute-start.6) | collective-permute-done | bytes 786464 | tf_op jit(solution)/shard_map/ppermute | solution.py:34
  112.3 1.2 constant_dynamic-update-slice_fusion.5
  113.5 16.6 %collective-permute-done.7 = bf16[128,3072]{1,0:T(8,128)(2,1)S(1)} collective-permute-done((bf16[128,3072]{1,0:T(8,128)(2,1)S(1)}, bf16[128,3072]{1,0:T(8,128)(2,1)S(1)}, u32[]{:S(2)}, u32[]{:S(2)}) %collective-permute-start.7) | collective-permute-done | bytes 786464 | tf_op jit(solution)/shard_map/ppermute | solution.py:34
  130.1 1.2 constant_dynamic-update-slice_fusion.4
  131.5 15.8 %collective-permute-done.8 = bf16[128,3072]{1,0:T(8,128)(2,1)S(1)} collective-permute-done((bf16[128,3072]{1,0:T(8,128)(2,1)S(1)}, bf16[128,3072]{1,0:T(8,128)(2,1)S(1)}, u32[]{:S(2)}, u32[]{:S(2)}) %collective-permute-start.8) | collective-permute-done | bytes 786464 | tf_op jit(solution)/shard_map/ppermute | solution.py:34
  147.3 3.7 fusion.19
  151.0 1.6 copy-done.1
  152.8 4.7 gather_fusion.2
  157.5 7.2 %broadcast_select_fusion.1 = bf16[8,2,128,2048]{3,2,1,0:T(8,128)(2,1)} fusion(bf16[8,2,128,2048]{3,2,1,0:T(8,128)(2,1)} %bitcast.120, pred[8,2]{1,0:T(8,128)(4,1)S(1)} %copy.22), kind=kLoop, calls=%fused_computation.39 | loop fusion | flops 4194304 | bytes 16777232 | tf_op jit(solution)/shard_map/jit(_where)/select_n | solution.py:123
  164.7 5.1 all-to-all-start
  171.1 2.3 slice.39
  173.4 199.3 %all-to-all-done = bf16[8,2,128,2048]{3,2,1,0:T(8,128)(2,1)} async-done(((bf16[8,2,128,2048]{3,2,1,0:T(8,128)(2,1)}), bf16[8,2,128,2048]{3,2,1,0:T(8,128)(2,1)}, u32[]{:S(2)}, u32[]{:S(2)}) %all-to-all-start) | async-done | bytes 8388640 | tf_op jit(solution)/shard_map/all_to_all | solution.py:126
  372.7 157.8 %while.12 = (s32[]{:T(128)}, bf16[4,128,1024]{2,1,0:T(8,128)(2,1)}, pred[4,6]{1,0:T(4,128)(4,1)S(1)}, s32[4,6]{1,0:T(4,128)S(1)}, bf16[16,128,2048]{2,1,0:T(8,12...) while((s32[]{:T(128)}, bf16[4,128,1024]{2,1,0:T(8,128)(2,1)}, ...), condition=%wide.region_6.7_spmd, body=%wide.region_3.6_spmd.sunk | while | flops 413804064 | bytes 59273044 | solution.py:139
  372.8 6.0 gather_fusion
  378.7 4.7 copy.33
  383.4 2.5 gather_fusion.1
  385.9 4.6 copy.34
  390.6 3.2 broadcast_select_fusion.5
  393.8 1.8 fusion.65
  395.7 1.0 constant_dynamic-slice_fusion.8
  398.7 6.4 %fusion.67 = (f32[16,128]{1,0:T(8,128)S(1)}, f32[16,128,768]{2,1,0:T(8,128)}) fusion(pred[768]{0:T(1024)(128)(4,1)S(1)} %fusion.66, bf16[128,16,64]{0,2,1:T(8,128)(2,1)} %bitcast.121, bf16[768,16,64]{0,2,1:T(8,128)(2,1)} %bitcast.119), kind=kOutput, calls=%fused_computation.97.clone.1 | convolution fusion | flops 207618816 | bytes 8135424 | tf_op jit(solution)/shard_map/while/body/eval_jaxpr/sub | solution.py:74
  405.1 5.3 fusion.68
  410.4 1.1 copy.36
  412.2 6.0 gather_fusion
  418.2 4.7 copy.33
  422.9 2.5 gather_fusion.1
  425.4 4.6 copy.34
  430.1 3.2 broadcast_select_fusion.5
  433.3 1.8 fusion.65
  435.1 1.0 constant_dynamic-slice_fusion.8
  438.2 6.4 %fusion.67 = (f32[16,128]{1,0:T(8,128)S(1)}, f32[16,128,768]{2,1,0:T(8,128)}) fusion(pred[768]{0:T(1024)(128)(4,1)S(1)} %fusion.66, bf16[128,16,64]{0,2,1:T(8,128)(2,1)} %bitcast.121, bf16[768,16,64]{0,2,1:T(8,128)(2,1)} %bitcast.119), kind=kOutput, calls=%fused_computation.97.clone.1 | convolution fusion | flops 207618816 | bytes 8135424 | tf_op jit(solution)/shard_map/while/body/eval_jaxpr/sub | solution.py:74
  444.5 5.3 fusion.68
  449.8 1.1 copy.36
  451.7 6.0 gather_fusion
  457.6 4.7 copy.33
  462.3 2.5 gather_fusion.1
  464.8 4.6 copy.34
  469.5 3.2 broadcast_select_fusion.5
  472.7 1.8 fusion.65
  474.6 1.0 constant_dynamic-slice_fusion.8
  477.6 6.4 %fusion.67 = (f32[16,128]{1,0:T(8,128)S(1)}, f32[16,128,768]{2,1,0:T(8,128)}) fusion(pred[768]{0:T(1024)(128)(4,1)S(1)} %fusion.66, bf16[128,16,64]{0,2,1:T(8,128)(2,1)} %bitcast.121, bf16[768,16,64]{0,2,1:T(8,128)(2,1)} %bitcast.119), kind=kOutput, calls=%fused_computation.97.clone.1 | convolution fusion | flops 207618816 | bytes 8135424 | tf_op jit(solution)/shard_map/while/body/eval_jaxpr/sub | solution.py:74
  484.0 5.3 fusion.68
  489.3 1.1 copy.36
  491.1 6.0 gather_fusion
  497.1 4.7 copy.33
  501.8 2.5 gather_fusion.1
  504.3 4.6 copy.34
  509.0 3.2 broadcast_select_fusion.5
  512.2 1.8 fusion.65
  514.0 1.0 constant_dynamic-slice_fusion.8
  517.0 6.4 %fusion.67 = (f32[16,128]{1,0:T(8,128)S(1)}, f32[16,128,768]{2,1,0:T(8,128)}) fusion(pred[768]{0:T(1024)(128)(4,1)S(1)} %fusion.66, bf16[128,16,64]{0,2,1:T(8,128)(2,1)} %bitcast.121, bf16[768,16,64]{0,2,1:T(8,128)(2,1)} %bitcast.119), kind=kOutput, calls=%fused_computation.97.clone.1 | convolution fusion | flops 207618816 | bytes 8135424 | tf_op jit(solution)/shard_map/while/body/eval_jaxpr/sub | solution.py:74
  523.4 5.3 fusion.68
  528.7 1.1 copy.36
  530.5 4.0 convolution_convert_fusion.1
  535.4 4.1 fusion.24
  539.5 61.7 %reduce-scatter.2.cloned.1.call-done = bf16[128,1024]{1,0:T(8,128)(2,1)} async-done(((bf16[1024,1024]{1,0:T(8,128)(2,1)}), bf16[128,1024]{1,0:T(8,128)(2,1)}) %reduce-scatter.2.cloned.1.call-update) | async-done | bytes 262160 | tf_op jit(solution)/shard_map/reduce_scatter | solution.py:142
  601.2 1.1 fusion.32
  602.3 2.1 conditional.4
  602.4 1.9 collective-permute-done
  (97 shorter events, 18.2 us)
Async XLA Ops:
  7.2 523.4 %copy-start = (bf16[1,512,1024]{2,1,0:T(8,128)(2,1)S(1)}, bf16[1,512,1024]{2,1,0:T(8,128)(2,1)}, u32[]{:S(2)}) copy-start(bf16[1,512,1024]{2,1,0:T(8,128)(2,1)} %param.13) | copy-start | bytes 3145732
  7.2 86.7 %copy-start.3 = (bf16[1,128,3072]{2,1,0:T(8,128)(2,1)S(1)}, bf16[1,128,3072]{2,1,0:T(8,128)(2,1)}, u32[]{:S(2)}) copy-start(bf16[1,128,3072]{2,1,0:T(8,128)(2,1)} %param.14) | copy-start | bytes 2359300
  7.2 23.8 %collective-permute-start.2 = (bf16[128,3072]{1,0:T(8,128)(2,1)}, bf16[128,3072]{1,0:T(8,128)(2,1)S(1)}, u32[]{:S(2)}, u32[]{:S(2)}) collective-permute-start(bf16[128,3072]{1,0:T(8,128)(2,1)} %bitcast.124), channel_id=1, source_target_pairs={{0,1},{1,2},{2,3},{3,4},{4,5},{5,6},{6,7},{7,0},{8,9},{9,10},{10,1... | collective-permute-start | bytes 2359304 | tf_op jit(solution)/shard_map/ppermute | solution.py:34
  31.0 21.4 %collective-permute-start.3 = (bf16[128,3072]{1,0:T(8,128)(2,1)S(1)}, bf16[128,3072]{1,0:T(8,128)(2,1)S(1)}, u32[]{:S(2)}, u32[]{:S(2)}) collective-permute-start(bf16[128,3072]{1,0:T(8,128)(2,1)S(1)} %collective-permute-done.2), channel_id=1, source_target_pairs={{0,1},{1,2},{2,3},{3,4},{4,5},{5,6},{6,7},{7,0},{8,9},{9,10},{10,1... | collective-permute-start | bytes 2359304 | tf_op jit(solution)/shard_map/ppermute | solution.py:34
  52.4 20.7 %collective-permute-start.4 = (bf16[128,3072]{1,0:T(8,128)(2,1)S(1)}, bf16[128,3072]{1,0:T(8,128)(2,1)}, u32[]{:S(2)}, u32[]{:S(2)}) collective-permute-start(bf16[128,3072]{1,0:T(8,128)(2,1)S(1)} %collective-permute-done.3), channel_id=1, source_target_pairs={{0,1},{1,2},{2,3},{3,4},{4,5},{5,6},{6,7},{7,0},{8,9},{9,10},{10,1... | collective-permute-start | bytes 2359304 | tf_op jit(solution)/shard_map/ppermute | solution.py:34
  73.1 20.0 %collective-permute-start.5 = (bf16[128,3072]{1,0:T(8,128)(2,1)}, bf16[128,3072]{1,0:T(8,128)(2,1)}, u32[]{:S(2)}, u32[]{:S(2)}) collective-permute-start(bf16[128,3072]{1,0:T(8,128)(2,1)} %collective-permute-done.4), channel_id=1, source_target_pairs={{0,1},{1,2},{2,3},{3,4},{4,5},{5,6},{6,7},{7,0},{8,9},{9,10},{10,1... | collective-permute-start | bytes 2359304 | tf_op jit(solution)/shard_map/ppermute | solution.py:34
  93.1 19.0 %collective-permute-start.6 = (bf16[128,3072]{1,0:T(8,128)(2,1)}, bf16[128,3072]{1,0:T(8,128)(2,1)S(1)}, u32[]{:S(2)}, u32[]{:S(2)}) collective-permute-start(bf16[128,3072]{1,0:T(8,128)(2,1)} %collective-permute-done.5), channel_id=1, source_target_pairs={{0,1},{1,2},{2,3},{3,4},{4,5},{5,6},{6,7},{7,0},{8,9},{9,10},{10,1... | collective-permute-start | bytes 2359304 | tf_op jit(solution)/shard_map/ppermute | solution.py:34
  93.9 53.4 %copy-start.5 = (bf16[1,512,1024]{2,1,0:T(8,128)(2,1)S(1)}, bf16[1,512,1024]{2,1,0:T(8,128)(2,1)}, u32[]{:S(2)}) copy-start(bf16[1,512,1024]{2,1,0:T(8,128)(2,1)} %param.12) | copy-start | bytes 3145732
  112.1 18.0 %collective-permute-start.7 = (bf16[128,3072]{1,0:T(8,128)(2,1)S(1)}, bf16[128,3072]{1,0:T(8,128)(2,1)S(1)}, u32[]{:S(2)}, u32[]{:S(2)}) collective-permute-start(bf16[128,3072]{1,0:T(8,128)(2,1)S(1)} %collective-permute-done.6), channel_id=1, source_target_pairs={{0,1},{1,2},{2,3},{3,4},{4,5},{5,6},{6,7},{7,0},{8,9},{9,10},{10,1... | collective-permute-start | bytes 2359304 | tf_op jit(solution)/shard_map/ppermute | solution.py:34
  130.1 17.1 %collective-permute-start.8 = (bf16[128,3072]{1,0:T(8,128)(2,1)S(1)}, bf16[128,3072]{1,0:T(8,128)(2,1)S(1)}, u32[]{:S(2)}, u32[]{:S(2)}) collective-permute-start(bf16[128,3072]{1,0:T(8,128)(2,1)S(1)} %collective-permute-done.7), channel_id=1, source_target_pairs={{0,1},{1,2},{2,3},{3,4},{4,5},{5,6},{6,7},{7,0},{8,9},{9,10},{10,1... | collective-permute-start | bytes 2359304 | tf_op jit(solution)/shard_map/ppermute | solution.py:34
  151.0 1.6 copy-start.1
  164.7 6.4 %copy-start.7 = (s32[1,32]{1,0:T(1,128)S(1)}, s32[1,32]{1,0:T(1,128)}, u32[]{:S(2)}) copy-start(s32[1,32]{1,0:T(1,128)} %param.18) | copy-start | bytes 388
  164.7 208.1 %all-to-all-start = ((bf16[8,2,128,2048]{3,2,1,0:T(8,128)(2,1)}), bf16[8,2,128,2048]{3,2,1,0:T(8,128)(2,1)}, u32[]{:S(2)}, u32[]{:S(2)}) async-start(bf16[8,2,128,2048]{3,2,1,0:T(8,128)(2,1)} %broadcast_select_fusion.1), calls=%async_computation | async-start | bytes 16777216 | tf_op jit(solution)/shard_map/all_to_all | solution.py:126
  169.8 365.6 %all-gather.3.cloned.1.call-start = ((), (), s32[]{:S(2)}) async-start(), calls=%async_computation.3 | async-start | bytes 2359296 | tf_op jit(solution)/shard_map/all_gather | solution.py:140
  170.5 430.6 %reduce-scatter.2.cloned.1.call-start = ((), (), s32[]{:S(2)}) async-start(), calls=%async_computation.2 | async-start | bytes 2359296 | tf_op jit(solution)/shard_map/reduce_scatter | solution.py:142
  530.5 4.8 copy-start.6
  534.5 66.6 %copy-start.2 = (bf16[1,128,1024]{2,1,0:T(8,128)(2,1)S(1)}, bf16[1,128,1024]{2,1,0:T(8,128)(2,1)}, u32[]{:S(2)}) copy-start(bf16[1,128,1024]{2,1,0:T(8,128)(2,1)} %param.15) | copy-start | bytes 786436
  534.5 66.6 %copy-start.4 = (f32[1,128,1024]{2,1,0:T(8,128)S(1)}, f32[1,128,1024]{2,1,0:T(8,128)}, u32[]{:S(2)}) copy-start(f32[1,128,1024]{2,1,0:T(8,128)} %param.16) | copy-start | bytes 1572868
  602.3 2.0 collective-permute-start
Sparse Core Ops, SparseCore 0:
  172.7 164.8 all-gather.2
  534.6 66.4 reduce-scatter.1
